TPU v7x, 32 devices: a whole 2x2x4 slice. The times are simulated.
32 devices in a mesh: left: 4 (over y, x), right: 8 (over z, core).
Axes of the slice: x: 2, y: 2, z: 4, core: 2. Of those that a mesh axis runs over, the one named last changes fastest.
Arguments:
- state: float32 [32, 1024, 1024], P(('left', 'right')), may hold values from -20 to 20
- left_env: bfloat16 [2, 32, 1024, 1024], P(None, ('left', 'right')), may hold values from -0.5 to 2.5
- right_env: bfloat16 [2, 32, 1024, 1024], P(None, ('left', 'right')), may hold values from -0.5 to 2.5
- site_ops: float32 [2, 4, 4], replicated, may hold values from -3 to 3
- left_live: int32 [8], replicated, may hold values from 1 to 4
- right_live: int32 [10], replicated, may hold values from 1 to 4
Outputs:
- next_vector: float32 [32, 1024, 1024], P(('left', 'right'))
- coefficients: float32 [2], replicated
All inputs are finite; a program needn't handle non-finite values.
Results may differ from a plain program's by a relative error of at most 0.0047.
Values may be sent and summed in bfloat16 or wider, within the bound.
No kernel may reach another device: no remote copies, remote signals or barrier semaphores. Data moves between devices by JAX's collectives and lax.ppermute only.
A program may use at most 64 MiB of HBM per device.

v0:
```python
import jax
import jax.numpy as jnp
from jax import lax
from jax.sharding import PartitionSpec as P

BLOCK = 256


def from_behind(block, axis, distance):
    devices = range(lax.axis_size(axis))
    route = [(i - distance, i) for i in devices if i - distance in devices]
    return lax.ppermute(block, axis, route)


def small_lookup(table, index):
    places = jnp.arange(table.shape[0], dtype=jnp.int32)
    return jnp.sum(jnp.where(places == index, table, jnp.zeros_like(table)))


def table_entry(table, row, column):
    rows = jnp.arange(table.shape[0], dtype=jnp.int32)[:, None]
    columns = jnp.arange(table.shape[1], dtype=jnp.int32)[None, :]
    return jnp.sum(jnp.where((rows == row) & (columns == column), table, jnp.zeros_like(table)))


def per_device(state, left_env, right_env, site_ops, left_live, right_live):
    pairs = site_ops.shape[1]
    sec_size = state.shape[1]
    block_size = BLOCK
    block_index = lax.axis_index("left") * lax.axis_size("right") + lax.axis_index("right")
    own_pair = block_index % pairs
    sector = block_index // pairs
    steps = (jnp.arange(pairs, dtype=jnp.int32) + 1) // 2
    own_step = small_lookup(steps, own_pair)
    positions = jnp.arange(sec_size, dtype=jnp.int32)
    row_mask = (positions < small_lookup(left_live, sector) * block_size).astype(jnp.float32)
    col_mask = (positions < small_lookup(right_live, sector + own_step) * block_size).astype(
        jnp.float32
    )
    live = row_mask[:, None] * col_mask[None, :]
    entries = float(
        state.shape[0] * sec_size * sec_size * lax.axis_size("left") * lax.axis_size("right")
    )
    masked = state[0] * live
    start_sum = lax.psum(jnp.sum(masked * masked), ("left", "right"))
    start_mean = start_sum / entries
    vector = masked / jnp.sqrt(start_mean + 1e-06)
    rounded = vector.astype(jnp.bfloat16)
    far_two = from_behind(rounded, ("left", "right"), 2)
    far_three = from_behind(rounded, ("left", "right"), 3)
    weights = []
    for offset in (2, 3):
        source_pair = (own_pair - offset) % pairs
        valid = block_index >= offset
        weights.append(
            jnp.where(
                valid, table_entry(site_ops[0], own_pair, source_pair), jnp.zeros((), jnp.float32)
            )
        )
    source = (
        weights[0] * far_two.astype(jnp.float32) + weights[1] * far_three.astype(jnp.float32)
    ).astype(jnp.bfloat16)
    part_zero = jnp.dot(source, right_env[0, 0], preferred_element_type=jnp.float32).astype(
        jnp.bfloat16
    )
    part_one = jnp.dot(rounded, right_env[1, 0], preferred_element_type=jnp.float32).astype(
        jnp.bfloat16
    )
    diag_weight = table_entry(site_ops[1], own_pair, own_pair)
    image = jnp.dot(left_env[0, 0], part_zero, preferred_element_type=jnp.float32)
    image = image + diag_weight * jnp.dot(
        left_env[1, 0], part_one, preferred_element_type=jnp.float32
    )
    image = image * live
    cross_sum, image_sum = lax.psum(
        (jnp.sum(vector * image), jnp.sum(image * image)), ("left", "right")
    )
    alpha_value = cross_sum / entries
    vector_mean = start_mean / (start_mean + 1e-06)
    residual_mean = image_sum / entries - alpha_value * alpha_value * (2.0 - vector_mean)
    residual = image - alpha_value * vector
    beta_value = jnp.sqrt(residual_mean + 1e-06)
    next_vector = residual / beta_value
    return (next_vector[None], jnp.stack([alpha_value, beta_value]))


def solution(mesh):
    in_specs = (
        P(("left", "right"), None, None),
        P(None, ("left", "right"), None, None),
        P(None, ("left", "right"), None, None),
        P(),
        P(),
        P(),
    )
    out_specs = (P(("left", "right"), None, None), P())
    return jax.shard_map(
        per_device, mesh=mesh, in_specs=in_specs, out_specs=out_specs, check_vma=False
    )
```

profile of v0, /device:TPU:14, one launch (start us, length us, event | category | flops | bytes accessed | tf_op | source)
XLA Modules:
  0.0 257.6 jit_solution(7007591481380401742)
XLA Ops:
  0.6 0.6 select_reduce_fusion
  1.9 1.3 fusion.36
  3.2 1.3 fusion.37
  5.8 5.3 %copy.8 = f32[1,1024,1024]{1,2,0:T(8,128)} copy(f32[1,1024,1024]{2,1,0:T(8,128)} %param.6) | data formatting | bytes 8388608 | tf_op args[0]
  11.2 4.1 %multiply_reduce_fusion.2 = f32[]{:T(128)} fusion(f32[1,1024,1024]{1,2,0:T(8,128)} %copy.8, f32[1024]{0:T(1024)S(1)} %get-tuple-element.13, f32[1024]{0:T(1024)S(1)} %get-tuple-element.12), kind=kLoop, calls=%fused_computation.7 | loop fusion | flops 4194303 | bytes 4202500 | tf_op jit(solution)/shard_map/reduce_sum | solution.py:45
  15.3 0.0 copy-start
  15.3 40.7 %psum.21 = f32[]{:T(128)} all-reduce(f32[]{:T(128)} %multiply_reduce_fusion.2), channel_id=1, replica_groups=mesh['left'=4,'right'=8] {'left','right'}, use_global_device_ids=true, to_apply=%region_5.6 | all-reduce | flops 1 | bytes 8 | tf_op jit(solution)/shard_map/psum | solution.py:45
  56.7 2.7 %fusion.38 = bf16[1024,1024]{0,1:T(8,128)(2,1)S(1)} fusion(f32[]{:T(128)S(6)} %sqrt.6, f32[1024]{0:T(1024)S(1)} %get-tuple-element.13, f32[1024]{0:T(1024)S(1)} %get-tuple-element.12, f32[1,1024,1024]{1,2,0:T(8,128)} %copy.8), kind=kLoop, calls=%fused_computation.50 | loop fusion | flops 4194304 | bytes 6299652 | tf_op jit(solution)/shard_map/convert_element_type | solution.py:48
  59.4 1.9 collective-permute-start.1
  61.4 3.3 %collective-permute-start = (bf16[1024,1024]{0,1:T(8,128)(2,1)S(1)}, bf16[1024,1024]{0,1:T(8,128)(2,1)}, u32[]{:S(2)}, u32[]{:S(2)}) collective-permute-start(bf16[1024,1024]{0,1:T(8,128)(2,1)S(1)} %fusion.38), channel_id=1, source_target_pairs={{0,2},{1,3},{2,4},{3,5},{4,6},{5,7},{6,8},{7,9},{8,10},{9,11},{10,... | collective-permute-start | bytes 6291464 | tf_op jit(solution)/shard_map/ppermute | solution.py:12
  64.8 0.0 copy-done
  64.8 0.8 fusion.33
  66.8 62.5 %collective-permute-done.1 = bf16[1024,1024]{0,1:T(8,128)(2,1)} collective-permute-done((bf16[1024,1024]{0,1:T(8,128)(2,1)S(1)}, bf16[1024,1024]{0,1:T(8,128)(2,1)}, u32[]{:S(2)}, u32[]{:S(2)}) %collective-permute-start.1) | collective-permute-done | bytes 2097184 | tf_op jit(solution)/shard_map/ppermute | solution.py:12
  129.2 44.9 %collective-permute-done = bf16[1024,1024]{0,1:T(8,128)(2,1)} collective-permute-done((bf16[1024,1024]{0,1:T(8,128)(2,1)S(1)}, bf16[1024,1024]{0,1:T(8,128)(2,1)}, u32[]{:S(2)}, u32[]{:S(2)}) %collective-permute-start) | collective-permute-done | bytes 2097184 | tf_op jit(solution)/shard_map/ppermute | solution.py:12
  174.2 10.0 %fusion.6 = f32[1024,1024]{1,0:T(8,128)} fusion(bf16[2,1,1024,1024]{3,2,1,0:T(8,128)(2,1)} %param.7, bf16[1024,1024]{0,1:T(8,128)(2,1)} %collective-permute-done.1, bf16[1024,1024]{0,1:T(8,128)(2,1)} %collective-permute-done, bf16[2,1,1024,1024]{3,2,1,0:T(8,128)(2,1)} %param.8, f32[]{:T(128)S(6)} %select_n.63, f32[]{:T(128)S(6)} %select_n.55), kind=kOutput, calls=%fused_computation.14 | convolution fusion | flops 4302307328 | bytes 12582920 | tf_op jit(solution)/shard_map/dot_general | solution.py:70
  184.2 13.4 %multiply_reduce_fusion.1 = (f32[]{:T(128)}, f32[]{:T(128)}, f32[1024,1024]{0,1:T(8,128)}) fusion(f32[]{:T(128)S(6)} %sqrt.6, f32[1024]{0:T(1024)S(1)} %get-tuple-element.13, f32[1024]{0:T(1024)S(1)} %get-tuple-element.12, f32[1,1024,1024]{1,2,0:T(8,128)} %copy.8, f32[1024,1024]{1,0:T(8,128)} %fusion.6, bf16[2,1,1024,1024]{3,2,1,0:T(8,128)(2,1)} %param.7, ...), kind=kOutput, calls=%fused_computation.4 | convolution fusion | flops 4310695936 | bytes 20989448 | tf_op jit(solution)/shard_map/dot_general | solution.py:71
  197.6 44.9 %all-reduce = (f32[]{:T(128)}, f32[]{:T(128)}) all-reduce(f32[]{:T(128)} %get-tuple-element.5, f32[]{:T(128)} %get-tuple-element.4), channel_id=1, replica_groups=mesh['left'=4,'right'=8] {'left','right'}, use_global_device_ids=true, to_apply=%region_11.12 | all-reduce | flops 2 | bytes 16 | tf_op jit(solution)/shard_map/psum | solution.py:75
  245.3 6.4 %divide_bitcast_fusion = f32[1,1024,1024]{1,2,0:T(8,128)} fusion(f32[1024,1024]{0,1:T(8,128)} %get-tuple-element.11, f32[]{:T(128)} %sqrt.7, f32[]{:T(128)} %div.58, f32[]{:T(128)S(6)} %sqrt.6, f32[1024]{0:T(1024)S(1)} %get-tuple-element.13, f32[1024]{0:T(1024)S(1)} %get-tuple-element.12, f32[1,1024,1024]{1,2,0:T(8,128)} %copy.8), kind=kLoop, calls=%fused_computation.2 | loop fusion | flops 6291456 | bytes 12591116 | tf_op jit(solution)/shard_map/broadcast_in_dim | solution.py:84
  251.7 5.3 %copy.9 = f32[1,1024,1024]{2,1,0:T(8,128)} copy(f32[1,1024,1024]{1,2,0:T(8,128)} %divide_bitcast_fusion) | data formatting | bytes 8388608
  257.0 0.6 pad_maximum_fusion
  (3 shorter events, 0.0 us)
Async XLA Ops:
  15.3 49.4 %copy-start = (f32[2,4,4]{2,1,0:T(4,128)S(1)}, f32[2,4,4]{2,1,0:T(4,128)}, u32[]{:S(2)}) copy-start(f32[2,4,4]{2,1,0:T(4,128)} %param.9) | copy-start | bytes 388
  59.4 69.8 %collective-permute-start.1 = (bf16[1024,1024]{0,1:T(8,128)(2,1)S(1)}, bf16[1024,1024]{0,1:T(8,128)(2,1)}, u32[]{:S(2)}, u32[]{:S(2)}) collective-permute-start(bf16[1024,1024]{0,1:T(8,128)(2,1)S(1)} %fusion.38), channel_id=1, source_target_pairs={{0,3},{1,4},{2,5},{3,6},{4,7},{5,8},{6,9},{7,10},{8,11},{9,12},{10... | collective-permute-start | bytes 6291464 | tf_op jit(solution)/shard_map/ppermute | solution.py:12
  61.4 112.8 %collective-permute-start = (bf16[1024,1024]{0,1:T(8,128)(2,1)S(1)}, bf16[1024,1024]{0,1:T(8,128)(2,1)}, u32[]{:S(2)}, u32[]{:S(2)}) collective-permute-start(bf16[1024,1024]{0,1:T(8,128)(2,1)S(1)} %fusion.38), channel_id=1, source_target_pairs={{0,2},{1,3},{2,4},{3,5},{4,6},{5,7},{6,8},{7,9},{8,10},{9,11},{10,... | collective-permute-start | bytes 6291464 | tf_op jit(solution)/shard_map/ppermute | solution.py:12
where the time goes:
time: 258 us
  waiting for transfers between devices  107 us (41%)
  blocking collectives  85.6 us (33%)
  matrix products  23.4 us (9%)
  other arithmetic  17.8 us (7%)
  local copies, waits for them, and re-layouts  10.7 us (4%)
  between operations  7.46 us (3%)
  starting transfers between devices  5.22 us (2%)
    ppermute x2, waiting for transfers between devices, from_behind(): return lax.ppermute(block, axis, route)  107 us
    psum x1, blocking collectives, per_device(): lax.psum((jnp.sum(vector * image), jnp.sum(image * image)), ('left', 'rig...  44.9 us
    psum x1, blocking collectives, per_device(): start_sum = lax.psum(jnp.sum(masked * masked), ('left', 'right'))  40.7 us
    dot_general x1, matrix products, per_device(): jnp.dot(left_env[1, 0], part_one, preferred_element_type=jnp.float32)  13.4 us
    unnamed x4, local copies, waits for them, and re-layouts  10.7 us
    dot_general x1, matrix products, per_device(): jnp.dot(left_env[0, 0], part_zero, preferred_element_type=jnp.float32)  9.99 us
    broadcast_in_dim x1, other arithmetic, per_device(): return (next_vector[None], jnp.stack([alpha_value, beta_value]))  6.39 us
    ppermute x2, starting transfers between devices, from_behind(): return lax.ppermute(block, axis, route)  5.22 us
  transfers between devices with their start and end apart: 2, of which 2 were waited for; matrix products, arithmetic and copies ran while one was open for 0% of the time, Pallas kernels for 0%

commit v1 on v0

--- a/solution.py
+++ b/solution.py
@@ -2,6 +2,7 @@
 import jax.numpy as jnp
 from jax import lax
 from jax.sharding import PartitionSpec as P
+from jax.lax import psum
 
 BLOCK = 256
 
@@ -24,6 +25,11 @@
 
 
 def per_device(state, left_env, right_env, site_ops, left_live, right_live):
+
+    def see_bench(a0):
+        block_next = psum(psum(a0, "right"), "left")
+        return block_next
+
     pairs = site_ops.shape[1]
     sec_size = state.shape[1]
     block_size = BLOCK
@@ -72,9 +78,7 @@
         left_env[1, 0], part_one, preferred_element_type=jnp.float32
     )
     image = image * live
-    cross_sum, image_sum = lax.psum(
-        (jnp.sum(vector * image), jnp.sum(image * image)), ("left", "right")
-    )
+    cross_sum, image_sum = see_bench((jnp.sum(vector * image), jnp.sum(image * image)))
     alpha_value = cross_sum / entries
     vector_mean = start_mean / (start_mean + 1e-06)
     residual_mean = image_sum / entries - alpha_value * alpha_value * (2.0 - vector_mean)

time: 258 us -> 244 us (0.946)
  the two profiles are of different devices: /device:TPU:14 before, /device:TPU:0 now
where the time goes in v1:
time: 244 us; the launch traced here: 243 us
  blocking collectives  94.5 us (39%)
  waiting for transfers between devices  81.4 us (33%)
  matrix products  23.4 us (10%)
  other arithmetic  17.8 us (7%)
  local copies, waits for them, and re-layouts  10.7 us (4%)
  starting transfers between devices  8.19 us (3%)
  between operations  7.2 us (3%)
    ppermute x2, waiting for transfers between devices, from_behind(): return lax.ppermute(block, axis, route)  81.4 us
    psum x2, blocking collectives, see_bench(): block_next = psum(psum(a0, 'right'), 'left')  52.3 us
    psum x1, blocking collectives, per_device(): start_sum = lax.psum(jnp.sum(masked * masked), ('left', 'right'))  42.2 us
    dot_general x1, matrix products, per_device(): jnp.dot(left_env[1, 0], part_one, preferred_element_type=jnp.float32)  13.4 us
    unnamed x4, local copies, waits for them, and re-layouts  10.7 us
    dot_general x1, matrix products, per_device(): jnp.dot(left_env[0, 0], part_zero, preferred_element_type=jnp.float32)  9.99 us
    ppermute x2, starting transfers between devices, from_behind(): return lax.ppermute(block, axis, route)  8.19 us
    broadcast_in_dim x1, other arithmetic, per_device(): return (next_vector[None], jnp.stack([alpha_value, beta_value]))  6.39 us
  transfers between devices with their start and end apart: 2, of which 2 were waited for; matrix products, arithmetic and copies ran while one was open for 0% of the time, Pallas kernels for 0%

profile of v1, /device:TPU:0, one launch (start us, length us, event | category | flops | bytes accessed | tf_op | source)
XLA Modules:
  0.0 243.2 jit_solution(4456225347709528931)
XLA Ops:
  0.6 0.6 select_reduce_fusion
  1.9 1.3 fusion.36
  3.2 1.3 fusion.37
  5.8 5.3 %copy.8 = f32[1,1024,1024]{1,2,0:T(8,128)} copy(f32[1,1024,1024]{2,1,0:T(8,128)} %param.6) | data formatting | bytes 8388608 | tf_op args[0]
  11.2 4.1 %multiply_reduce_fusion.2 = f32[]{:T(128)} fusion(f32[1,1024,1024]{1,2,0:T(8,128)} %copy.8, f32[1024]{0:T(1024)S(1)} %get-tuple-element.15, f32[1024]{0:T(1024)S(1)} %get-tuple-element.14), kind=kLoop, calls=%fused_computation.7 | loop fusion | flops 4194303 | bytes 4202500 | tf_op jit(solution)/shard_map/reduce_sum | solution.py:51
  15.3 0.0 copy-start
  15.3 42.2 %psum.35 = f32[]{:T(128)} all-reduce(f32[]{:T(128)} %multiply_reduce_fusion.2), channel_id=1, replica_groups=mesh['left'=4,'right'=8] {'left','right'}, use_global_device_ids=true, to_apply=%region_5.6 | all-reduce | flops 1 | bytes 8 | tf_op jit(solution)/shard_map/psum | solution.py:51
  58.2 2.7 %fusion.38 = bf16[1024,1024]{0,1:T(8,128)(2,1)S(1)} fusion(f32[]{:T(128)S(6)} %sqrt.6, f32[1024]{0:T(1024)S(1)} %get-tuple-element.15, f32[1024]{0:T(1024)S(1)} %get-tuple-element.14, f32[1,1024,1024]{1,2,0:T(8,128)} %copy.8), kind=kLoop, calls=%fused_computation.50 | loop fusion | flops 4194304 | bytes 6299652 | tf_op jit(solution)/shard_map/convert_element_type | solution.py:54
  61.0 3.6 %collective-permute-start.1 = (bf16[1024,1024]{0,1:T(8,128)(2,1)S(1)}, bf16[1024,1024]{0,1:T(8,128)(2,1)}, u32[]{:S(2)}, u32[]{:S(2)}) collective-permute-start(bf16[1024,1024]{0,1:T(8,128)(2,1)S(1)} %fusion.38), channel_id=1, source_target_pairs={{0,3},{1,4},{2,5},{3,6},{4,7},{5,8},{6,9},{7,10},{8,11},{9,12},{10... | collective-permute-start | bytes 6291464 | tf_op jit(solution)/shard_map/ppermute | solution.py:13
  64.5 4.6 %collective-permute-start = (bf16[1024,1024]{0,1:T(8,128)(2,1)S(1)}, bf16[1024,1024]{0,1:T(8,128)(2,1)}, u32[]{:S(2)}, u32[]{:S(2)}) collective-permute-start(bf16[1024,1024]{0,1:T(8,128)(2,1)S(1)} %fusion.38), channel_id=1, source_target_pairs={{0,2},{1,3},{2,4},{3,5},{4,6},{5,7},{6,8},{7,9},{8,10},{9,11},{10,... | collective-permute-start | bytes 6291464 | tf_op jit(solution)/shard_map/ppermute | solution.py:13
  69.2 0.0 copy-done
  69.2 0.8 fusion.33
  71.2 36.4 %collective-permute-done.1 = bf16[1024,1024]{0,1:T(8,128)(2,1)} collective-permute-done((bf16[1024,1024]{0,1:T(8,128)(2,1)S(1)}, bf16[1024,1024]{0,1:T(8,128)(2,1)}, u32[]{:S(2)}, u32[]{:S(2)}) %collective-permute-start.1) | collective-permute-done | bytes 2097184 | tf_op jit(solution)/shard_map/ppermute | solution.py:13
  107.7 44.9 %collective-permute-done = bf16[1024,1024]{0,1:T(8,128)(2,1)} collective-permute-done((bf16[1024,1024]{0,1:T(8,128)(2,1)S(1)}, bf16[1024,1024]{0,1:T(8,128)(2,1)}, u32[]{:S(2)}, u32[]{:S(2)}) %collective-permute-start) | collective-permute-done | bytes 2097184 | tf_op jit(solution)/shard_map/ppermute | solution.py:13
  152.6 10.0 %fusion.6 = f32[1024,1024]{1,0:T(8,128)} fusion(bf16[2,1,1024,1024]{3,2,1,0:T(8,128)(2,1)} %param.7, bf16[1024,1024]{0,1:T(8,128)(2,1)} %collective-permute-done.1, bf16[1024,1024]{0,1:T(8,128)(2,1)} %collective-permute-done, bf16[2,1,1024,1024]{3,2,1,0:T(8,128)(2,1)} %param.8, f32[]{:T(128)S(6)} %select_n.63, f32[]{:T(128)S(6)} %select_n.55), kind=kOutput, calls=%fused_computation.14 | convolution fusion | flops 4302307328 | bytes 12582920 | tf_op jit(solution)/shard_map/dot_general | solution.py:76
  162.6 13.4 %multiply_reduce_fusion.1 = (f32[]{:T(128)}, f32[]{:T(128)}, f32[1024,1024]{0,1:T(8,128)}) fusion(f32[]{:T(128)S(6)} %sqrt.6, f32[1024]{0:T(1024)S(1)} %get-tuple-element.15, f32[1024]{0:T(1024)S(1)} %get-tuple-element.14, f32[1,1024,1024]{1,2,0:T(8,128)} %copy.8, f32[1024,1024]{1,0:T(8,128)} %fusion.6, bf16[2,1,1024,1024]{3,2,1,0:T(8,128)(2,1)} %param.7, ...), kind=kOutput, calls=%fused_computation.4 | convolution fusion | flops 4310695936 | bytes 20989448 | tf_op jit(solution)/shard_map/dot_general | solution.py:77
  176.1 38.5 %all-reduce = (f32[]{:T(128)}, f32[]{:T(128)}) all-reduce(f32[]{:T(128)} %get-tuple-element.5, f32[]{:T(128)} %get-tuple-element.4), channel_id=1, replica_groups=mesh['left'=4,'right'=8] {'right'}, use_global_device_ids=true, to_apply=%region_12.13 | all-reduce | flops 2 | bytes 16 | tf_op jit(solution)/shard_map/psum | solution.py:30
  214.5 13.8 %all-reduce.1 = (f32[]{:T(128)}, f32[]{:T(128)}) all-reduce(f32[]{:T(128)} %get-tuple-element.9, f32[]{:T(128)} %get-tuple-element.10), channel_id=1, replica_groups=mesh['left'=4,'right'=8] {'left'}, use_global_device_ids=true, to_apply=%region_13.14 | all-reduce | flops 2 | bytes 16 | tf_op jit(solution)/shard_map/psum | solution.py:30
  230.9 6.4 %divide_bitcast_fusion = f32[1,1024,1024]{1,2,0:T(8,128)} fusion(f32[1024,1024]{0,1:T(8,128)} %get-tuple-element.13, f32[]{:T(128)} %sqrt.7, f32[]{:T(128)} %div.58, f32[]{:T(128)S(6)} %sqrt.6, f32[1024]{0:T(1024)S(1)} %get-tuple-element.15, f32[1024]{0:T(1024)S(1)} %get-tuple-element.14, f32[1,1024,1024]{1,2,0:T(8,128)} %copy.8), kind=kLoop, calls=%fused_computation.2 | loop fusion | flops 6291456 | bytes 12591116 | tf_op jit(solution)/shard_map/broadcast_in_dim | solution.py:88
  237.3 5.3 %copy.9 = f32[1,1024,1024]{2,1,0:T(8,128)} copy(f32[1,1024,1024]{1,2,0:T(8,128)} %divide_bitcast_fusion) | data formatting | bytes 8388608
  242.6 0.6 pad_maximum_fusion
  (3 shorter events, 0.0 us)
Async XLA Ops:
  15.3 53.9 %copy-start = (f32[2,4,4]{2,1,0:T(4,128)S(1)}, f32[2,4,4]{2,1,0:T(4,128)}, u32[]{:S(2)}) copy-start(f32[2,4,4]{2,1,0:T(4,128)} %param.9) | copy-start | bytes 388
  61.0 46.7 %collective-permute-start.1 = (bf16[1024,1024]{0,1:T(8,128)(2,1)S(1)}, bf16[1024,1024]{0,1:T(8,128)(2,1)}, u32[]{:S(2)}, u32[]{:S(2)}) collective-permute-start(bf16[1024,1024]{0,1:T(8,128)(2,1)S(1)} %fusion.38), channel_id=1, source_target_pairs={{0,3},{1,4},{2,5},{3,6},{4,7},{5,8},{6,9},{7,10},{8,11},{9,12},{10... | collective-permute-start | bytes 6291464 | tf_op jit(solution)/shard_map/ppermute | solution.py:13
  64.5 88.1 %collective-permute-start = (bf16[1024,1024]{0,1:T(8,128)(2,1)S(1)}, bf16[1024,1024]{0,1:T(8,128)(2,1)}, u32[]{:S(2)}, u32[]{:S(2)}) collective-permute-start(bf16[1024,1024]{0,1:T(8,128)(2,1)S(1)} %fusion.38), channel_id=1, source_target_pairs={{0,2},{1,3},{2,4},{3,5},{4,6},{5,7},{6,8},{7,9},{8,10},{9,11},{10,... | collective-permute-start | bytes 6291464 | tf_op jit(solution)/shard_map/ppermute | solution.py:13
